TPU v7x, 256 devices: a whole 4x4x8 slice. The times are simulated.
256 devices in a mesh: dp: 4 (over y), head: 4 (over x), seq: 16 (over z, core).
Axes of the slice: x: 4, y: 4, z: 8, core: 2. Of those that a mesh axis runs over, the one named last changes fastest.
Arguments:
- q_dense: bfloat16 [32768, 8, 128], P(('dp', 'seq'), 'head'), parts along dimension 0, may hold values from -108 to 108
- k_dense: bfloat16 [32768, 8, 128], P(('dp', 'seq'), 'head'), parts along dimension 0, may hold values from -4 to 4
- v_dense: bfloat16 [32768, 8, 128], P(('dp', 'seq'), 'head'), parts along dimension 0, may hold values from -4 to 4
- q_expert: bfloat16 [32768, 12, 128], P(('dp', 'seq'), 'head'), parts along dimension 0, may hold values from -108 to 108
- k_expert: bfloat16 [32768, 12, 128], P(('dp', 'seq'), 'head'), parts along dimension 0, may hold values from -4 to 4
- v_expert: bfloat16 [32768, 12, 128], P(('dp', 'seq'), 'head'), parts along dimension 0, may hold values from -4 to 4
- gate_logit: bfloat16 [12, 32768], P('head', ('dp', 'seq')), parts along dimension 1, may hold values from -8 to 8
- selection: int32 [12, 2048], P('head', 'dp'), parts along dimension 1, may hold values from 0 to 8191, as said below
Outputs:
- dense_out: bfloat16 [32768, 8, 128], P(('dp', 'seq'), 'head'), parts along dimension 0
- expert_out: bfloat16 [32768, 12, 128], P(('dp', 'seq'), 'head'), parts along dimension 0
There are 4 independent parts, one for each index of `dp`. A program takes and returns all parts, laid end to end along the dimension named above; each array names one. Nothing has to cross between parts.
Inputs may be any that keep to these rules, and one draw needn't show every extreme that they name: `selection`: each row lists 512 distinct token positions in increasing order; every row holds the first and the last token.
All inputs are finite; a program needn't handle non-finite values.
Results may differ from a plain program's by a relative error of at most 0.0055.
Values may be sent and summed in bfloat16 or wider, within the bound.
No kernel may reach another device: no remote copies, remote signals or barrier semaphores. Data moves between devices by JAX's collectives and lax.ppermute only.
A program may use at most 64 MiB of HBM per device.

v0:
```python
import math
import jax
import jax.numpy as jnp
from jax import lax
from jax.sharding import PartitionSpec as P

NEGATIVE = -1e30


def plain_rows(rows, tok_rows, count):
    return rows


def online_update(state, queries, query_pos, keys, values, key_pos, scale):
    leading, total, summed = state
    scores = jnp.einsum("qhd,khd->qhk", queries, keys, preferred_element_type=jnp.float32) * scale
    visible = key_pos[None, None, :] <= query_pos[:, None, None]
    scores = jnp.where(visible, scores, NEGATIVE)
    new_leading = jnp.maximum(leading, jnp.max(scores, axis=2))
    shrink = jnp.exp(leading - new_leading)
    weights = jnp.where(visible, jnp.exp(scores - new_leading[:, :, None]), 0.0)
    total = total * shrink + jnp.sum(weights, axis=2)
    moved = jnp.einsum(
        "qhk,khd->qhd", weights.astype(jnp.bfloat16), values, preferred_element_type=jnp.float32
    )
    return (new_leading, total, summed * shrink[:, :, None] + moved)


def dense_heads(queries, keys, values, position_map):
    tok_rows, heads, width = queries.shape
    count = lax.axis_size("seq")
    half_rows = tok_rows // 2
    own_rows = lax.axis_index("seq") * tok_rows + jnp.arange(tok_rows, dtype=jnp.int32)
    query_pos = position_map(own_rows, tok_rows, count).reshape(2, half_rows)
    groups = queries.reshape(2, half_rows, heads, width)
    scale = 1.0 / math.sqrt(width)
    blank = (
        jnp.full((half_rows, heads), NEGATIVE, jnp.float32),
        jnp.zeros((half_rows, heads), jnp.float32),
        jnp.zeros((half_rows, heads, width), jnp.float32),
    )
    key_rows = lax.all_gather(keys, "seq", axis=0, tiled=True)
    value_rows = lax.all_gather(values, "seq", axis=0, tiled=True)
    length = key_rows.shape[0]
    block = math.gcd(length, 512)
    count_blocks = length // block
    key_pos = position_map(jnp.arange(length, dtype=jnp.int32), tok_rows, count).reshape(
        count_blocks, block
    )
    key_blocks = key_rows.reshape(count_blocks, block, heads, width)
    value_blocks = value_rows.reshape(count_blocks, block, heads, width)

    def advance(state, item):
        key_block, value_block, block_pos = item
        result = []
        for group in range(2):
            seen = jnp.min(block_pos) <= jnp.max(query_pos[group])
            result.append(
                lax.cond(
                    seen,
                    lambda inner, member=group: online_update(
                        inner,
                        groups[member],
                        query_pos[member],
                        key_block,
                        value_block,
                        block_pos,
                        scale,
                    ),
                    lambda inner: inner,
                    state[group],
                )
            )
        return (tuple(result), None)

    final_state, unused = lax.scan(advance, (blank, blank), (key_blocks, value_blocks, key_pos))
    outputs = [
        (summed / total[:, :, None]).astype(jnp.bfloat16) for leading, total, summed in final_state
    ]
    return jnp.concatenate(outputs, axis=0)


def attend_ranked(query_rows, query_ranks, keys, values, gate_rows):
    heads, rows, width = query_rows.shape
    block = math.gcd(rows, 512)
    scale = 1.0 / math.sqrt(width)
    key_ranks = jnp.arange(keys.shape[1], dtype=jnp.int32)

    def one_block(index):
        scores = (
            jnp.einsum("erd,ekd->erk", query_rows, keys, preferred_element_type=jnp.float32) * scale
        )
        visible = key_ranks[None, None, :] <= query_ranks[:, :, None]
        scores = jnp.where(visible, scores, NEGATIVE)
        leading = jnp.max(scores, axis=2, keepdims=True)
        weights = jnp.where(visible, jnp.exp(scores - leading), 0.0)
        total = jnp.sum(weights, axis=2, keepdims=True)
        mixed = (
            jnp.einsum(
                "erk,ekd->erd",
                weights.astype(jnp.bfloat16),
                values,
                preferred_element_type=jnp.float32,
            )
            / total
        )
        return (mixed * jax.nn.sigmoid(gate_rows.astype(jnp.float32))[:, :, None]).astype(
            jnp.bfloat16
        )

    blocks = lax.map(one_block, jnp.arange(rows // block, dtype=jnp.int32))
    return jnp.moveaxis(blocks, 0, 1).reshape(heads, rows, width)


def sparse_heads(queries, keys, values, gate_logit, selection):
    tok_rows, heads, width = queries.shape
    chosen = selection.shape[1]
    start = lax.axis_index("seq") * tok_rows
    positions = start + jnp.arange(tok_rows, dtype=jnp.int32)
    matches = selection[:, :, None] == positions[None, None, :]
    one_hot = matches.astype(jnp.bfloat16)

    def pick(source):
        return jnp.einsum(
            "ent,ted->end", one_hot, source, preferred_element_type=jnp.float32
        ).astype(jnp.bfloat16)

    gate_rows = jnp.einsum("ent,et->en", one_hot, gate_logit, preferred_element_type=jnp.float32)
    gathered = (
        lax.psum(pick(queries), "seq").astype(jnp.float32),
        lax.psum(pick(keys), "seq").astype(jnp.float32),
        lax.psum(pick(values), "seq").astype(jnp.float32),
        lax.psum(gate_rows.astype(jnp.bfloat16), "seq").astype(jnp.float32),
    )
    picked_q, picked_k, picked_v, picked_gate = [member.astype(jnp.bfloat16) for member in gathered]
    all_ranks = jnp.broadcast_to(jnp.arange(chosen, dtype=jnp.int32)[None, :], (heads, chosen))
    results = attend_ranked(picked_q, all_ranks, picked_k, picked_v, picked_gate)
    return jnp.einsum("ent,end->ted", one_hot, results, preferred_element_type=jnp.float32).astype(
        jnp.bfloat16
    )


def local(q_dense, k_dense, v_dense, q_expert, k_expert, v_expert, gate_logit, selection):
    dense_out = dense_heads(q_dense, k_dense, v_dense, plain_rows)
    expert_out = sparse_heads(q_expert, k_expert, v_expert, gate_logit, selection)
    return (dense_out, expert_out)


def solution(mesh):
    placed = (
        P(("dp", "seq"), "head", None),
        P(("dp", "seq"), "head", None),
        P(("dp", "seq"), "head", None),
        P(("dp", "seq"), "head", None),
        P(("dp", "seq"), "head", None),
        P(("dp", "seq"), "head", None),
        P("head", ("dp", "seq")),
        P("head", "dp"),
    )
    return jax.shard_map(
        local,
        mesh=mesh,
        in_specs=placed,
        out_specs=(P(("dp", "seq"), "head", None), P(("dp", "seq"), "head", None)),
        check_vma=False,
    )
```

profile of v0, /device:TPU:225, one launch (start us, length us, event | category | flops | bytes accessed | tf_op | source)
XLA Modules:
  0.0 332.1 jit_solution(16076033150022781153)
XLA Ops:
  8.2 2.1 fusion.67
  10.3 2.5 fusion.61
  12.7 1.4 fusion.64
  16.6 23.1 %psum.31 = bf16[3,512]{1,0:T(4,128)(2,1)S(1)} all-reduce(bf16[3,512]{1,0:T(4,128)(2,1)S(1)} %bitcast.68), channel_id=1, replica_groups=mesh['dp'=4,'head'=4,'seq'=16] {'seq'}, use_global_device_ids=true, to_apply=%region_18.19 | all-reduce | flops 1536 | bytes 6144 | tf_op jit(solution)/shard_map/psum | solution.py:133
  40.3 87.0 %all-reduce.3.cloned.1.call-done = (bf16[3,512,128]{2,1,0:T(8,128)(2,1)}, bf16[3,512,128]{2,1,0:T(8,128)(2,1)}, bf16[3,512,128]{2,1,0:T(8,128)(2,1)}) async-done(((bf16[3,512,128]{2,1,0:T(8,128)(2,1)}, bf16[3,512,128]{2,1,0:T(8,128)(2,1)}, bf16[3,512,128]{2,1,0:T(8,128)(2,1)}), (bf16[3,512,128]{2,1,0:T(8,128)(2,1)}, bf16[3,512,128]{2,1,0:T(8,128)(2,1)}, ...) | async-done | bytes 1179664 | tf_op jit(solution)/shard_map/psum | solution.py:132
  127.3 2.1 fusion.90
  129.5 1.6 fusion.73
  132.0 39.2 %all-gather.3.cloned.1.call-done = bf16[8192,2,128]{2,0,1:T(8,128)(2,1)} async-done(((bf16[512,2,128]{2,0,1:T(8,128)(2,1)}), bf16[8192,2,128]{2,0,1:T(8,128)(2,1)}) %all-gather.3.cloned.1.call-update) | async-done | bytes 4194320 | tf_op jit(solution)/shard_map/all_gather | solution.py:42
  171.2 42.6 %all-gather.5.cloned.1.call-done = bf16[8192,2,128]{2,0,1:T(8,128)(2,1)} async-done(((bf16[512,2,128]{2,0,1:T(8,128)(2,1)}), bf16[8192,2,128]{2,0,1:T(8,128)(2,1)}) %all-gather.5.cloned.1.call-update) | async-done | bytes 4194320 | tf_op jit(solution)/shard_map/all_gather | solution.py:43
  213.9 109.1 %while.26 = (s32[]{:T(128)}, f32[256,2]{0,1:T(2,128)S(1)}, f32[256,2]{0,1:T(2,128)S(1)}, f32[256,2,128]{2,0,1:T(8,128)S(1)}, f32[256,2]{0,1:T(2,128)S(1)}, /*ind...) while((s32[]{:T(128)}, f32[256,2]{0,1:T(2,128)S(1)}, ...), condition=%wide.region_12.13_spmd.clone, body=%wide.region_2.12_spmd.clone.sunk | while | flops 273682432 | bytes 10830257 | solution.py:76
  215.9 1.1 dynamic-slice_bitcast_fusion.3
  217.0 1.3 conditional.6
  219.4 1.3 conditional.7
  222.7 1.1 dynamic-slice_bitcast_fusion.3
  223.8 1.3 conditional.6
  226.3 1.3 conditional.7
  229.5 1.1 dynamic-slice_bitcast_fusion.3
  230.6 1.3 conditional.6
  233.1 1.3 conditional.7
  236.3 1.1 dynamic-slice_bitcast_fusion.3
  237.4 1.3 conditional.6
  239.9 1.3 conditional.7
  244.2 1.3 conditional.6
  246.7 1.3 conditional.7
  250.0 1.1 dynamic-slice_bitcast_fusion.3
  251.0 1.3 conditional.6
  253.5 1.3 conditional.7
  257.9 1.3 conditional.6
  260.3 1.3 conditional.7
  264.7 1.3 conditional.6
  267.2 1.3 conditional.7
  271.5 1.3 conditional.6
  274.0 1.3 conditional.7
  278.3 1.3 conditional.6
  280.8 1.3 conditional.7
  285.1 1.3 conditional.6
  287.6 1.3 conditional.7
  291.9 1.3 conditional.6
  294.4 1.3 conditional.7
  298.8 1.3 conditional.6
  301.2 1.3 conditional.7
  305.6 1.3 conditional.6
  308.1 1.3 conditional.7
  312.4 1.3 conditional.6
  314.9 1.3 conditional.7
  319.2 1.3 conditional.6
  321.7 1.3 conditional.7
  323.3 1.2 fusion.82
  (341 shorter events, 67.6 us)
Async XLA Ops:
  7.2 1.0 copy-start
  7.2 5.6 %copy-start.6 = (s32[3,512]{1,0:T(4,128)S(1)}, s32[3,512]{1,0:T(4,128)}, u32[]{:S(2)}) copy-start(s32[3,512]{1,0:T(4,128)} %param.21) | copy-start | bytes 18436
  7.2 5.5 %copy-start.4 = (bf16[512,3,128]{2,0,1:T(8,128)(2,1)S(1)}, bf16[512,3,128]{2,0,1:T(8,128)(2,1)}, u32[]{:S(2)}) copy-start(bf16[512,3,128]{2,0,1:T(8,128)(2,1)} %param.18) | copy-start | bytes 1179652
  7.2 120.1 %all-reduce.3.cloned.1.call-start = ((), (), s32[]{:S(2)}) async-start(), calls=%async_computation.2 | async-start | bytes 2359296 | tf_op jit(solution)/shard_map/psum | solution.py:132
  10.3 4.0 %copy-start.1 = (bf16[512,2,128]{2,1,0:T(2,128)(2,1)S(1)}, bf16[512,2,128]{2,1,0:T(2,128)(2,1)}, u32[]{:S(2)}) copy-start(bf16[512,2,128]{2,1,0:T(2,128)(2,1)} %param.15) | copy-start | bytes 786436
  10.3 4.8 %copy-start.2 = (bf16[512,2,128]{2,1,0:T(2,128)(2,1)S(1)}, bf16[512,2,128]{2,1,0:T(2,128)(2,1)}, u32[]{:S(2)}) copy-start(bf16[512,2,128]{2,1,0:T(2,128)(2,1)} %param.16) | copy-start | bytes 786436
  10.3 5.6 %copy-start.3 = (bf16[512,2,128]{2,1,0:T(2,128)(2,1)S(1)}, bf16[512,2,128]{2,1,0:T(2,128)(2,1)}, u32[]{:S(2)}) copy-start(bf16[512,2,128]{2,1,0:T(2,128)(2,1)} %param.14) | copy-start | bytes 786436
  12.7 3.2 copy-start.7
  14.2 157.1 %all-gather.3.cloned.1.call-start = ((), (), s32[]{:S(2)}) async-start(), calls=%async_computation | async-start | bytes 4456448 | tf_op jit(solution)/shard_map/all_gather | solution.py:42
  15.0 198.9 %all-gather.5.cloned.1.call-start = ((), (), s32[]{:S(2)}) async-start(), calls=%async_computation.1 | async-start | bytes 4456448 | tf_op jit(solution)/shard_map/all_gather | solution.py:43
  127.3 2.1 copy-start.5
Sparse Core Ops, SparseCore 0:
  14.3 113.0 all-reduce.2
  129.8 41.4 all-gather.2
  173.1 40.6 all-gather.4
where the time goes:
time: 333 us; the launch traced here: 332 us
  waiting for transfers between devices  169 us (51%)
  loops' own time  42.3 us (13%)
  matrix products  36.9 us (11%)
  other arithmetic  25.7 us (8%)
  blocking collectives  23.1 us (7%)
  local copies, waits for them, and re-layouts  21.1 us (6%)
  between operations  13.9 us (4%)
    psum x1, waiting for transfers between devices, sparse_heads(): lax.psum(pick(values), 'seq').astype(jnp.float32)  87 us
    all_gather x1, waiting for transfers between devices, dense_heads(): value_rows = lax.all_gather(values, 'seq', axis=0, tiled=True)  42.6 us
    another operation x1, loops' own time, dense_heads(): lax.scan(advance, (blank, blank), (key_blocks, value_blocks, key_pos))  40.4 us
    all_gather x1, waiting for transfers between devices, dense_heads(): key_rows = lax.all_gather(keys, 'seq', axis=0, tiled=True)  39.2 us
    psum x1, blocking collectives, sparse_heads(): lax.psum(gate_rows.astype(jnp.bfloat16), 'seq').astype(jnp.float32)  23.1 us
    squeeze x16, local copies, waits for them, and re-layouts, dense_heads(): lax.scan(advance, (blank, blank), (key_blocks, value_blocks, key_pos))  17.2 us
    dot_general x32, matrix products, online_update(): jnp.einsum('qhk,khd->qhd', weights.astype(jnp.bfloat16), values, preferre...  16.5 us
    reduce_min x16, other arithmetic, advance(): seen = jnp.min(block_pos) <= jnp.max(query_pos[group])  10.3 us
  transfers between devices with their start and end apart: 3, of which 3 were waited for; matrix products, arithmetic and copies ran while one was open for 2% of the time, Pallas kernels for 0%

commit v1 on v0

--- a/solution.py
+++ b/solution.py
@@ -5,6 +5,12 @@
 from jax.sharding import PartitionSpec as P
 
 NEGATIVE = -1e30
+
+
+def gather_by_exchange(x, axis, dim):
+    size = lax.axis_size(axis)
+    repeats = [size if d == dim else 1 for d in range(x.ndim)]
+    return lax.all_to_all(jnp.tile(x, repeats), axis, split_axis=dim, concat_axis=dim, tiled=True)
 
 
 def plain_rows(rows, tok_rows, count):
@@ -39,7 +45,7 @@
         jnp.zeros((half_rows, heads), jnp.float32),
         jnp.zeros((half_rows, heads, width), jnp.float32),
     )
-    key_rows = lax.all_gather(keys, "seq", axis=0, tiled=True)
+    key_rows = gather_by_exchange(keys, "seq", 0)
     value_rows = lax.all_gather(values, "seq", axis=0, tiled=True)
     length = key_rows.shape[0]
     block = math.gcd(length, 512)

time: 333 us -> 365 us (1.096)
  blocking collectives: 23.1 us -> 113 us
  waiting for transfers between devices: 169 us -> 81.3 us
  local copies, waits for them, and re-layouts: 21.1 us -> 42.8 us
  starting transfers between devices: 0.12 us -> 6.38 us
    psum x1, blocking collectives: 23.1 us -> 113 us  [sparse_heads(): lax.psum(gate_rows.astype(jnp.bfloat16), 'seq').astype(jnp.float32)]
    psum x1, waiting for transfers between devices: 87 us -> 42 us  [sparse_heads(): lax.psum(pick(values), 'seq').astype(jnp.float32)]
    all_gather x1 -> x0, waiting for transfers between devices: 39.2 us -> none  [dense_heads(): key_rows = lax.all_gather(keys, 'seq', axis=0, tiled=True)]
    dynamic_slice x0 -> x32, local copies, waits for them, and re-layouts: none -> 18.8 us  [dense_heads(): lax.scan(advance, (blank, blank), (key_blocks, value_blocks, key_pos))]
    all_to_all x0 -> x1, starting transfers between devices: none -> 6.31 us  [gather_by_exchange(): lax.all_to_all(jnp.tile(x, repeats), axis, split_axis=dim, concat_axis=di...]
    another operation x0 -> x1, local copies, waits for them, and re-layouts: none -> 5.21 us  [gather_by_exchange(): jnp.tile(x, repeats)]
  transfers between devices with their start and end apart: 3 -> 3, of which waited for: 3 -> 2; matrix products, arithmetic and copies ran while one was open for 2% -> 3% of each run, Pallas kernels for 0% -> 0%
where the time goes in v1:
time: 365 us; the launch traced here: 363 us
  blocking collectives  113 us (31%)
  waiting for transfers between devices  81.3 us (22%)
  loops' own time  43.2 us (12%)
  local copies, waits for them, and re-layouts  42.8 us (12%)
  matrix products  36.9 us (10%)
  other arithmetic  25.7 us (7%)
  between operations  14.2 us (4%)
  starting transfers between devices  6.38 us (2%)
    psum x1, blocking collectives, sparse_heads(): lax.psum(gate_rows.astype(jnp.bfloat16), 'seq').astype(jnp.float32)  113 us
    psum x1, waiting for transfers between devices, sparse_heads(): lax.psum(pick(values), 'seq').astype(jnp.float32)  42 us
    another operation x1, loops' own time, dense_heads(): lax.scan(advance, (blank, blank), (key_blocks, value_blocks, key_pos))  41.3 us
    all_gather x1, waiting for transfers between devices, dense_heads(): value_rows = lax.all_gather(values, 'seq', axis=0, tiled=True)  39.3 us
    dynamic_slice x32, local copies, waits for them, and re-layouts, dense_heads(): lax.scan(advance, (blank, blank), (key_blocks, value_blocks, key_pos))  18.8 us
    dot_general x32, matrix products, online_update(): jnp.einsum('qhk,khd->qhd', weights.astype(jnp.bfloat16), values, preferre...  16.5 us
    squeeze x16, local copies, waits for them, and re-layouts, dense_heads(): lax.scan(advance, (blank, blank), (key_blocks, value_blocks, key_pos))  15.7 us
    reduce_min x16, other arithmetic, advance(): seen = jnp.min(block_pos) <= jnp.max(query_pos[group])  10.3 us
  transfers between devices with their start and end apart: 3, of which 2 were waited for; matrix products, arithmetic and copies ran while one was open for 3% of the time, Pallas kernels for 0%

profile of v1, /device:TPU:225, one launch (start us, length us, event | category | flops | bytes accessed | tf_op | source)
XLA Modules:
  0.0 363.5 jit_solution(12181003370883493377)
XLA Ops:
  8.2 2.1 fusion.67
  10.3 2.4 fusion.61
  12.7 1.4 fusion.64
  14.1 5.2 %tile.4 = bf16[16,512,2,128]{3,2,1,0:T(2,128)(2,1)} broadcast(bf16[512,2,128]{2,1,0:T(2,128)(2,1)S(1)} %copy-done.1), dimensions={1,2,3} | broadcast | bytes 4456448 | tf_op jit(solution)/shard_map/tile | solution.py:13
  19.3 6.3 %all-to-all-start = ((bf16[8192,2,128]{2,1,0:T(2,128)(2,1)}), bf16[8192,2,128]{2,1,0:T(2,128)(2,1)}, u32[]{:S(2)}, u32[]{:S(2)}) async-start(bf16[8192,2,128]{2,1,0:T(2,128)(2,1)} %bitcast.63), calls=%async_computation | async-start | bytes 8388608 | tf_op jit(solution)/shard_map/all_to_all | solution.py:13
  27.2 113.0 %psum.31 = bf16[3,512]{1,0:T(4,128)(2,1)S(1)} all-reduce(bf16[3,512]{1,0:T(4,128)(2,1)S(1)} %bitcast.72), channel_id=1, replica_groups=mesh['dp'=4,'head'=4,'seq'=16] {'seq'}, use_global_device_ids=true, to_apply=%region_18.19 | all-reduce | flops 1536 | bytes 6144 | tf_op jit(solution)/shard_map/psum | solution.py:139
  140.9 42.0 %all-reduce.3.cloned.1.call-done = (bf16[3,512,128]{2,1,0:T(8,128)(2,1)}, bf16[3,512,128]{2,1,0:T(8,128)(2,1)}, bf16[3,512,128]{2,1,0:T(8,128)(2,1)}) async-done(((bf16[3,512,128]{2,1,0:T(8,128)(2,1)}, bf16[3,512,128]{2,1,0:T(8,128)(2,1)}, bf16[3,512,128]{2,1,0:T(8,128)(2,1)}), (bf16[3,512,128]{2,1,0:T(8,128)(2,1)}, bf16[3,512,128]{2,1,0:T(8,128)(2,1)}, ...) | async-done | bytes 1179664 | tf_op jit(solution)/shard_map/psum | solution.py:138
  182.8 2.1 fusion.90
  185.0 1.6 fusion.73
  187.5 39.3 %all-gather.2.cloned.1.call-done = bf16[8192,2,128]{2,0,1:T(8,128)(2,1)} async-done(((bf16[512,2,128]{2,0,1:T(8,128)(2,1)}), bf16[8192,2,128]{2,0,1:T(8,128)(2,1)}) %all-gather.2.cloned.1.call-update) | async-done | bytes 4194320 | tf_op jit(solution)/shard_map/all_gather | solution.py:49
  226.9 127.2 %while.26 = (s32[]{:T(128)}, f32[256,2]{0,1:T(2,128)S(1)}, f32[256,2]{0,1:T(2,128)S(1)}, f32[256,2,128]{2,0,1:T(8,128)S(1)}, f32[256,2]{0,1:T(2,128)S(1)}, /*ind...) while((s32[]{:T(128)}, f32[256,2]{0,1:T(2,128)S(1)}, ...), condition=%wide.region_12.13_spmd.clone, body=%wide.region_2.12_spmd.clone.sunk | while | flops 273682432 | bytes 11354549 | solution.py:82
  228.8 1.1 constant_dynamic-slice_fusion.4
  231.0 1.3 conditional.6
  233.5 1.3 conditional.7
  236.7 1.1 constant_dynamic-slice_fusion.4
  238.9 1.3 conditional.6
  241.5 1.3 conditional.7
  244.7 1.1 constant_dynamic-slice_fusion.4
  246.9 1.3 conditional.6
  249.4 1.3 conditional.7
  252.6 1.1 constant_dynamic-slice_fusion.4
  254.8 1.3 conditional.6
  257.4 1.3 conditional.7
  262.8 1.3 conditional.6
  265.3 1.3 conditional.7
  270.7 1.3 conditional.6
  273.3 1.3 conditional.7
  278.7 1.3 conditional.6
  281.2 1.3 conditional.7
  286.6 1.3 conditional.6
  289.2 1.3 conditional.7
  294.6 1.3 conditional.6
  297.1 1.3 conditional.7
  302.5 1.3 conditional.6
  305.1 1.3 conditional.7
  310.5 1.3 conditional.6
  313.0 1.3 conditional.7
  318.4 1.3 conditional.6
  321.0 1.3 conditional.7
  326.4 1.3 conditional.6
  328.9 1.3 conditional.7
  334.3 1.3 conditional.6
  336.9 1.3 conditional.7
  342.3 1.3 conditional.6
  344.8 1.3 conditional.7
  350.2 1.3 conditional.6
  352.8 1.3 conditional.7
  354.3 1.2 fusion.82
  (372 shorter events, 84.9 us)
Async XLA Ops:
  7.2 1.0 copy-start
  7.2 5.5 %copy-start.6 = (s32[3,512]{1,0:T(4,128)S(1)}, s32[3,512]{1,0:T(4,128)}, u32[]{:S(2)}) copy-start(s32[3,512]{1,0:T(4,128)} %param.21) | copy-start | bytes 18436
  7.2 5.5 %copy-start.4 = (bf16[512,3,128]{2,0,1:T(8,128)(2,1)S(1)}, bf16[512,3,128]{2,0,1:T(8,128)(2,1)}, u32[]{:S(2)}) copy-start(bf16[512,3,128]{2,0,1:T(8,128)(2,1)} %param.18) | copy-start | bytes 1179652
  7.2 175.6 %all-reduce.3.cloned.1.call-start = ((), (), s32[]{:S(2)}) async-start(), calls=%async_computation.2 | async-start | bytes 2359296 | tf_op jit(solution)/shard_map/psum | solution.py:138
  10.3 3.9 %copy-start.1 = (bf16[512,2,128]{2,1,0:T(2,128)(2,1)S(1)}, bf16[512,2,128]{2,1,0:T(2,128)(2,1)}, u32[]{:S(2)}) copy-start(bf16[512,2,128]{2,1,0:T(2,128)(2,1)} %param.15) | copy-start | bytes 786436
  19.3 6.4 %copy-start.2 = (bf16[512,2,128]{2,1,0:T(2,128)(2,1)S(1)}, bf16[512,2,128]{2,1,0:T(2,128)(2,1)}, u32[]{:S(2)}) copy-start(bf16[512,2,128]{2,1,0:T(2,128)(2,1)} %param.16) | copy-start | bytes 786436
  19.3 7.1 %copy-start.3 = (bf16[512,2,128]{2,1,0:T(2,128)(2,1)S(1)}, bf16[512,2,128]{2,1,0:T(2,128)(2,1)}, u32[]{:S(2)}) copy-start(bf16[512,2,128]{2,1,0:T(2,128)(2,1)} %param.14) | copy-start | bytes 786436
  19.3 7.2 %copy-start.7 = (bf16[3,512]{1,0:T(4,128)(2,1)S(1)}, bf16[3,512]{1,0:T(4,128)(2,1)}, u32[]{:S(2)}) copy-start(bf16[3,512]{1,0:T(4,128)(2,1)} %param.20) | copy-start | bytes 9220
  19.3 168.2 %all-to-all-start = ((bf16[8192,2,128]{2,1,0:T(2,128)(2,1)}), bf16[8192,2,128]{2,1,0:T(2,128)(2,1)}, u32[]{:S(2)}, u32[]{:S(2)}) async-start(bf16[8192,2,128]{2,1,0:T(2,128)(2,1)} %bitcast.63), calls=%async_computation | async-start | bytes 8388608 | tf_op jit(solution)/shard_map/all_to_all | solution.py:13
  25.6 201.1 %all-gather.2.cloned.1.call-start = ((), (), s32[]{:S(2)}) async-start(), calls=%async_computation.1 | async-start | bytes 4456448 | tf_op jit(solution)/shard_map/all_gather | solution.py:49
  182.8 2.1 copy-start.5
Sparse Core Ops, SparseCore 0:
  14.2 168.5 all-reduce.2
  185.3 41.4 all-gather.1
